TPU v7x, 32 devices: a whole 2x2x4 slice. The times are simulated.
32 devices in a mesh: dp: 2 (over y), mp: 16 (over z, x, core).
Axes of the slice: x: 2, y: 2, z: 4, core: 2. Of those that a mesh axis runs over, the one named last changes fastest.
Arguments:
- queries: bfloat16 [2048, 1024], P(('dp', 'mp')), may hold values from -16 to 16
- hidden: bfloat16 [2048, 2048], P(('dp', 'mp')), may hold values from -6 to 6
- kv_pages: bfloat16 [192, 16, 2, 1024], P(('dp', 'mp')), may hold values from -8 to 8
- page_table: int32 [2, 96], replicated, may hold values from 0 to 191, as said below
- cache_len: int32 [2], replicated, may hold values from 1 to 512, as said below
- deal_table: int32 [2, 16], P('dp'), may hold values from 0 to 15, as said below
- out_weight: bfloat16 [1024, 2048], P('dp', 'mp'), may hold values from -0.1875 to 0.1875
- norm_gain: float32 [2048], replicated, may hold values from 0.1 to 1.9
- expert_ids: int32 [2048, 6], P(('dp', 'mp')), may hold values from 0 to 15, all different within a row; in each aligned block of 64 rows (0 to 63, 64 to 127, ...) at most 32 rows name the same one
- expert_gates: float32 [2048, 6], P(('dp', 'mp')), may hold values from 0.05 to 0.5
- experts_in: bfloat16 [16, 2048, 1408], P('mp', 'dp'), may hold values from -0.125 to 0.125
- experts_out: bfloat16 [16, 704, 2048], P('mp', None, 'dp'), may hold values from -0.21875 to 0.21875
Outputs:
- mixed: bfloat16 [2048, 2048], P(('dp', 'mp'))
Inputs may be any that keep to these rules, and one draw needn't show every extreme that they name: `deal_table`: each row is an ordering of 0 to 15: every piece of the 1 request of row d is held by one device of that row. For request r = d + j, the entries page_table[r, l] over all l are exactly the pages (d * 16 + m) * 6 + j * 6 + k for m < 16, k < 6, each once, in an order given by the draw. `cache_len`: some request has 512 cached tokens and some has 1. `expert_ids`: the 6 ids of a token differ; among the 64 tokens of one device no expert is named more than 32 times, and in some device one expert is named exactly 32 times.
All inputs are finite; a program needn't handle non-finite values.
Results may differ from a plain program's by a relative error of at most 0.0095.
Values may be sent and summed in bfloat16 or wider, within the bound.
No kernel may reach another device: no remote copies, remote signals or barrier semaphores. Data moves between devices by JAX's collectives and lax.ppermute only.
A program may use at most 128 MiB of HBM per device.

v0:
```python
import math
import jax
import jax.numpy as jnp
from jax import lax
from jax.sharding import PartitionSpec as P

HEADS = 8
HD = 128
TOPK = 6
PAGE = 16
epsilon = 1e-06


def attend_head(q_rows, key_rows, value_rows, key_pos, query_pos):
    scores = jnp.dot(q_rows, key_rows.T, preferred_element_type=jnp.float32) * (1.0 / math.sqrt(HD))
    allowed = key_pos[None, :] <= query_pos[:, None]
    scores = jnp.where(allowed, scores, -1e30)
    row_max = jnp.max(scores, axis=1, keepdims=True)
    weights = jnp.exp(scores - row_max)
    weights_bf = (weights / jnp.sum(weights, axis=1, keepdims=True)).astype(jnp.bfloat16)
    blended = jnp.dot(weights_bf, value_rows, preferred_element_type=jnp.float32)
    return blended.astype(jnp.bfloat16)


def swap_dp(x):
    return lax.ppermute(x, "dp", [(0, 1), (1, 0)])


def on_device(
    queries,
    hidden,
    kv_pages,
    page_table,
    cache_len,
    deal_table,
    out_weight,
    norm_gain,
    expert_ids,
    expert_gates,
    experts_in,
    experts_out,
):
    n_mp = lax.axis_size("mp")
    n_dp = lax.axis_size("dp")
    row_index = lax.axis_index("dp")
    column = lax.axis_index("mp")
    q_count = queries.shape[0]
    width = queries.shape[1]
    d_model = hidden.shape[1]
    heads = width // HD
    groups = n_mp // heads
    sub = q_count // groups
    my_head = column % heads
    my_group = column // heads
    page_share = page_table.shape[1] // n_mp
    pages_dev = kv_pages.shape[0]
    deal_row = deal_table[0]
    request = row_index
    page_count = page_table.shape[1]
    q_out = queries.reshape(sub, groups, heads, HD).transpose(1, 2, 0, 3).reshape(n_mp, sub, HD)
    kv_heads = kv_pages.reshape(pages_dev, PAGE, 2, heads, HD).transpose(3, 0, 1, 2, 4)
    kv_out = jnp.tile(kv_heads, (groups, 1, 1, 1, 1)).reshape(n_mp, pages_dev * PAGE * 2, HD)
    if n_dp == 2:
        w_pair = swap_dp(out_weight)
        wo_rows = jnp.where(
            row_index == 0,
            jnp.concatenate([out_weight, w_pair], axis=0),
            jnp.concatenate([w_pair, out_weight], axis=0),
        )
    else:
        wo_rows = lax.all_gather(out_weight, "dp", axis=0, tiled=True)
    bits = n_mp.bit_length() - 1
    kv_send = jnp.concatenate([q_out, kv_out], axis=1)
    if n_mp == 1 << bits:
        block = wo_rows[None]
        if bits > 2 and n_dp == 2:
            t1, t2 = (bits - 1, bits - 2)
            fetched = {}
            for a in range(2):
                for c in range(2):
                    off = a << t1 | c << t2
                    near = (
                        out_weight
                        if off == 0
                        else lax.ppermute(out_weight, "mp", [(m, m ^ off) for m in range(n_mp)])
                    )
                    other = lax.ppermute(
                        out_weight,
                        ("dp", "mp"),
                        [
                            (d * n_mp + m, (1 - d) * n_mp + (m ^ off))
                            for d in range(2)
                            for m in range(n_mp)
                        ],
                    )
                    fetched[a, c] = jnp.where(
                        row_index == 0,
                        jnp.concatenate([near, other], axis=0),
                        jnp.concatenate([other, near], axis=0),
                    )
            b1 = (column >> t1) % 2
            b2 = (column >> t2) % 2
            shards = []
            for x2 in range(2):
                for x3 in range(2):
                    a0 = b1 ^ x3 == 0
                    c0 = b2 ^ x2 == 0
                    shards.append(
                        jnp.where(
                            a0,
                            jnp.where(c0, fetched[0, 0], fetched[0, 1]),
                            jnp.where(c0, fetched[1, 0], fetched[1, 1]),
                        )
                    )
            block = jnp.stack(shards)
        elif bits > 1:
            b = bits - 1
            pair = lax.ppermute(block, "mp", [(m, m ^ 1 << b) for m in range(n_mp)])
            low = (column >> b) % 2 == 0
            block = jnp.concatenate(
                [jnp.where(low, block, pair), jnp.where(low, pair, block)], axis=0
            )
        block, kv_send = lax.optimization_barrier((block, kv_send))
    both = lax.all_to_all(kv_send, "mp", split_axis=0, concat_axis=0, tiled=True)
    q_in = both[:, :sub, :]
    arrived = both[:, sub:, :].reshape(n_mp, pages_dev, PAGE, 2, HD)
    first_pos = cache_len[request] + deal_row % n_mp * q_count
    query_pos = (
        first_pos[:, None] + jnp.arange(sub, dtype=jnp.int32)[None, :] * groups + my_group
    ).reshape(-1)
    slot_ids = jnp.arange(n_mp * page_share, dtype=jnp.int32)
    physical = (row_index * n_mp + slot_ids // page_share) * pages_dev + slot_ids % page_share
    table_row = page_table[request]
    matches = table_row[None, :] == physical[:, None]
    logical = jnp.sum(
        jnp.where(matches, jnp.arange(page_count, dtype=jnp.int32)[None, :], 0), axis=1
    )
    key_pos = (logical[:, None] * PAGE + jnp.arange(PAGE, dtype=jnp.int32)[None, :]).reshape(-1)
    key_rows = arrived[:, :, :, 0, :].reshape(-1, HD)
    value_rows = arrived[:, :, :, 1, :].reshape(-1, HD)
    blended = attend_head(q_in.reshape(-1, HD), key_rows, value_rows, key_pos, query_pos)
    back = lax.all_to_all(
        blended.reshape(n_mp, sub, HD), "mp", split_axis=0, concat_axis=0, tiled=True
    )
    attended = back.reshape(groups, heads, sub, HD).transpose(2, 0, 1, 3).reshape(q_count, width)
    bits = n_mp.bit_length() - 1
    if n_mp == 1 << bits:
        for b in reversed(range(1, bits - 2 if n_dp == 2 and bits > 2 else bits - 1)):
            pair = lax.ppermute(block, "mp", [(m, m ^ 1 << b) for m in range(n_mp)])
            low = (column >> b) % 2 == 0
            block = jnp.concatenate(
                [jnp.where(low, block, pair), jnp.where(low, pair, block)], axis=0
            )
        pair = lax.ppermute(block, "mp", [(m, m ^ 1) for m in range(n_mp)])
        own_part = jnp.einsum("tk,jkc->tjc", attended, block, preferred_element_type=jnp.float32)
        pair_part = jnp.einsum("tk,jkc->tjc", attended, pair, preferred_element_type=jnp.float32)
        low = column % 2 == 0
        by_shard = jnp.where(
            low,
            jnp.concatenate([own_part, pair_part], axis=1),
            jnp.concatenate([pair_part, own_part], axis=1),
        )
        order = (0,) + tuple(range(bits, 0, -1)) + (bits + 1,)
        shard_w = wo_rows.shape[1]
        projected = (
            by_shard.reshape((q_count,) + (2,) * bits + (shard_w,))
            .transpose(order)
            .reshape(q_count, d_model)
        )
    else:
        projected = jnp.dot(
            attended,
            lax.all_gather(wo_rows, "mp", axis=1, tiled=True),
            preferred_element_type=jnp.float32,
        )
    resid_f = (hidden.astype(jnp.float32) + projected).astype(jnp.bfloat16).astype(jnp.float32)
    mean_square = jnp.mean(resid_f * resid_f, axis=1, keepdims=True)
    normed = (resid_f * lax.rsqrt(mean_square + epsilon) * norm_gain[None, :]).astype(jnp.bfloat16)
    capacity = min(q_count, q_count * TOPK * 4 // (3 * n_mp))
    flat_ids = expert_ids.reshape(-1)
    one_hot = (flat_ids[:, None] == jnp.arange(n_mp, dtype=jnp.int32)[None, :]).astype(jnp.int32)
    slot_of = jnp.sum(jnp.cumsum(one_hot, axis=0) * one_hot, axis=1) - 1
    target = (flat_ids * capacity + slot_of).reshape(q_count, TOPK)
    hits = target[:, :, None] == jnp.arange(n_mp * capacity, dtype=jnp.int32)[None, None, :]
    dispatch = jnp.any(hits, axis=1).astype(jnp.bfloat16)
    combine = jnp.sum(jnp.where(hits, expert_gates[:, :, None], 0.0), axis=1)
    ff_width = experts_out.shape[1]
    if n_dp == 2:
        out_other = swap_dp(experts_out)
        in_other = swap_dp(experts_in)
        normed, out_other = lax.optimization_barrier((normed, out_other))
    sending = lax.dot_general(
        dispatch, normed, (((0,), (0,)), ((), ())), preferred_element_type=jnp.float32
    ).astype(jnp.bfloat16)
    received = lax.all_to_all(
        sending.reshape(n_mp, capacity, d_model), "mp", split_axis=0, concat_axis=0, tiled=True
    )
    flat_rows = received.reshape(-1, d_model)
    if n_dp == 2:
        first = row_index == 0
        gate_up = jnp.where(
            first,
            jnp.concatenate([experts_in[0], in_other[0]], axis=0),
            jnp.concatenate([in_other[0], experts_in[0]], axis=0),
        )
        down = jnp.where(
            first,
            jnp.concatenate([experts_out[0], out_other[0]], axis=1),
            jnp.concatenate([out_other[0], experts_out[0]], axis=1),
        )
        flat_rows, down, gate_up = lax.optimization_barrier((flat_rows, down, gate_up))
    else:
        gate_up = lax.all_gather(experts_in, "dp", axis=1, tiled=True)[0]
        down = lax.all_gather(experts_out, "dp", axis=2, tiled=True)[0]
    gate_vals = jnp.dot(flat_rows, gate_up, preferred_element_type=jnp.float32)
    act = (jax.nn.silu(gate_vals[:, :ff_width]) * gate_vals[:, ff_width:]).astype(jnp.bfloat16)
    outcome = jnp.dot(act, down, preferred_element_type=jnp.float32).astype(jnp.bfloat16)
    results = lax.all_to_all(
        outcome.reshape(n_mp, capacity, d_model), "mp", split_axis=0, concat_axis=0, tiled=True
    )
    expert_sum = jnp.dot(
        combine,
        results.reshape(-1, d_model).astype(jnp.float32),
        precision=lax.Precision.HIGHEST,
        preferred_element_type=jnp.float32,
    )
    return (resid_f + expert_sum).astype(jnp.bfloat16)


def solution(mesh):
    in_specs = (
        P(("dp", "mp"), None),
        P(("dp", "mp"), None),
        P(("dp", "mp"), None, None, None),
        P(),
        P(),
        P("dp", None),
        P("dp", "mp"),
        P(),
        P(("dp", "mp"), None),
        P(("dp", "mp"), None),
        P("mp", "dp", None),
        P("mp", None, "dp"),
    )
    out_specs = P(("dp", "mp"), None)
    return jax.shard_map(
        on_device, mesh=mesh, in_specs=in_specs, out_specs=out_specs, check_vma=False
    )
```

profile of v0, /device:TPU:11, one launch (start us, length us, event | category | flops | bytes accessed | tf_op | source)
XLA Modules:
  0.0 202.7 jit_solution(180145341147619317)
XLA Ops:
  0.0 2.3 %collective-permute-start.6 = (bf16[512,128]{1,0:T(8,128)(2,1)}, bf16[512,128]{1,0:T(8,128)(2,1)S(1)}, u32[]{:S(2)}, u32[]{:S(2)}) collective-permute-start(bf16[512,128]{1,0:T(8,128)(2,1)} %param.18), channel_id=1, source_target_pairs={{0,28},{1,29},{2,30},{3,31},{4,24},{5,25},{6,26},{7,27},{8,20},{9,... | collective-permute-start | bytes 393224 | tf_op jit(solution)/shard_map/ppermute | solution.py:87
  2.3 0.2 collective-permute-start
  2.5 2.2 %collective-permute-start.1 = (bf16[512,128]{1,0:T(8,128)(2,1)}, bf16[512,128]{1,0:T(8,128)(2,1)S(1)}, u32[]{:S(2)}, u32[]{:S(2)}) collective-permute-start(bf16[512,128]{1,0:T(8,128)(2,1)} %param.18), channel_id=1, source_target_pairs={{0,4},{1,5},{2,6},{3,7},{4,0},{5,1},{6,2},{7,3},{8,12},{9,13},{10,... | collective-permute-start | bytes 393224 | tf_op jit(solution)/shard_map/ppermute | solution.py:85
  4.7 1.0 collective-permute-start.2
  5.6 0.2 collective-permute-start.3
  5.9 0.8 copy.72
  6.7 0.1 eq.106
  6.8 0.9 reduce-window.6
  7.7 0.2 slice_reduce_fusion
  8.0 0.1 eq.102
  8.1 1.2 reshape.608
  9.4 0.3 copy.66
  9.7 0.9 copy.77
  10.8 2.2 %collective-permute-start.4 = (bf16[512,128]{1,0:T(8,128)(2,1)}, bf16[512,128]{1,0:T(8,128)(2,1)S(1)}, u32[]{:S(2)}, u32[]{:S(2)}) collective-permute-start(bf16[512,128]{1,0:T(8,128)(2,1)} %param.18), channel_id=1, source_target_pairs={{0,24},{1,25},{2,26},{3,27},{4,28},{5,29},{6,30},{7,31},{8,16},{9,... | collective-permute-start | bytes 393224 | tf_op jit(solution)/shard_map/ppermute | solution.py:87
  13.0 0.4 collective-permute-start.5
  13.4 0.6 tile.8
  14.0 1.0 pad_maximum_fusion.2
  15.0 1.1 collective-permute-start.9
  16.1 0.4 collective-permute-start.10
  16.4 7.3 %collective-permute-done.4 = bf16[512,128]{1,0:T(8,128)(2,1)S(1)} collective-permute-done((bf16[512,128]{1,0:T(8,128)(2,1)}, bf16[512,128]{1,0:T(8,128)(2,1)S(1)}, u32[]{:S(2)}, u32[]{:S(2)}) %collective-permute-start.4) | collective-permute-done | bytes 131104 | tf_op jit(solution)/shard_map/ppermute | solution.py:87
  23.8 3.7 %collective-permute-done.5 = bf16[512,128]{1,0:T(8,128)(2,1)S(1)} collective-permute-done((bf16[512,128]{1,0:T(8,128)(2,1)}, bf16[512,128]{1,0:T(8,128)(2,1)S(1)}, u32[]{:S(2)}, u32[]{:S(2)}) %collective-permute-start.5) | collective-permute-done | bytes 131104 | tf_op jit(solution)/shard_map/ppermute | solution.py:85
  27.5 0.3 broadcast_select_fusion.4
  27.7 0.3 broadcast_select_fusion.5
  28.0 0.3 broadcast_select_fusion.8
  28.3 0.3 broadcast_select_fusion.9
  28.6 0.1 pad_maximum_fusion.1
  28.8 0.3 collective-permute-start.7
  29.1 0.2 select_reduce_fusion.1
  29.3 0.6 dynamic_slice.7
  29.9 6.0 %all-to-all-start = ((bf16[16,224,128]{2,1,0:T(8,128)(2,1)}), bf16[16,224,128]{2,1,0:T(8,128)(2,1)S(1)}, u32[]{:S(2)}, u32[]{:S(2)}) async-start(bf16[16,224,128]{2,1,0:T(8,128)(2,1)} %pad_maximum_fusion.2), calls=%async_computation | async-start | bytes 1835008 | tf_op jit(solution)/shard_map/all_to_all | solution.py:124
  35.9 0.7 fusion.19
  36.7 23.9 %collective-permute-done.7 = bf16[4,1024,128]{2,1,0:T(8,128)(2,1)S(1)} collective-permute-done((bf16[4,1024,128]{2,1,0:T(8,128)(2,1)S(1)}, bf16[4,1024,128]{2,1,0:T(8,128)(2,1)S(1)}, u32[]{:S(2)}, u32[]{:S(2)}) %collective-permute-start.7) | collective-permute-done | bytes 1048608 | tf_op jit(solution)/shard_map/ppermute | solution.py:149
  60.6 0.1 broadcast_select_fusion.1
  60.8 0.2 pad_maximum_fusion
  61.0 2.0 collective-permute-start.8
  63.1 0.1 sub.29
  63.5 0.5 copy.67
  64.0 0.2 fusion.22
  64.2 0.1 copy.68
  64.3 0.1 copy.69
  64.4 0.7 fusion.23
  65.1 0.6 fusion.1
  65.7 1.4 fusion.5
  67.1 5.7 %all-to-all-start.1 = ((bf16[16,32,128]{2,1,0:T(8,128)(2,1)}), bf16[16,32,128]{2,1,0:T(8,128)(2,1)S(1)}, u32[]{:S(2)}, u32[]{:S(2)}) async-start(bf16[16,32,128]{2,1,0:T(8,128)(2,1)} %bitcast.19), calls=%async_computation.1 | async-start | bytes 262144 | tf_op jit(solution)/shard_map/all_to_all | solution.py:142
  72.8 0.2 fusion.8
  73.0 5.0 %all-to-all-done.1 = bf16[16,32,128]{2,1,0:T(8,128)(2,1)S(1)} async-done(((bf16[16,32,128]{2,1,0:T(8,128)(2,1)}), bf16[16,32,128]{2,1,0:T(8,128)(2,1)S(1)}, u32[]{:S(2)}, u32[]{:S(2)}) %all-to-all-start.1) | async-done | bytes 131104 | tf_op jit(solution)/shard_map/all_to_all | solution.py:142
  78.1 0.5 fusion.24
  78.6 2.1 %fusion.25 = f32[64,8,128]{2,0,1:T(8,128)S(1)} fusion(bf16[64,1024,1]{1,0,2:T(8,128)(2,1)S(1)} %reshape.620, bf16[8,1024,128]{2,1,0:T(8,128)(2,1)} %collective-permute-done.8), kind=kOutput, calls=%fused_computation.79 | convolution fusion | flops 134217728 | bytes 2490368 | tf_op jit(solution)/shard_map/tk,jkc->tjc/dot_general | solution.py:156
  80.8 0.4 copy.71
  81.2 0.4 reshape.614
  81.7 0.2 fusion.9
  81.8 0.1 fusion.11
  82.0 2.1 %convolution_convert_fusion.1 = bf16[512,2048]{1,0:T(8,128)(2,1)} fusion(pred[64,512]{1,0:T(8,128)(4,1)S(1)} %fusion.8, bf16[64,2048]{1,0:T(8,128)(2,1)S(1)} %fusion.11), kind=kOutput, calls=%fused_computation.6 | convolution fusion | flops 135266304 | bytes 2392064 | tf_op jit(solution)/shard_map/dot_general | solution.py:192
  84.1 7.1 %all-to-all-start.2 = ((bf16[16,32,2048]{2,1,0:T(8,128)(2,1)}), bf16[16,32,2048]{2,1,0:T(8,128)(2,1)}, u32[]{:S(2)}, u32[]{:S(2)}) async-start(bf16[16,32,2048]{2,1,0:T(8,128)(2,1)} %bitcast.25), calls=%async_computation.2 | async-start | bytes 4194304 | tf_op jit(solution)/shard_map/all_to_all | solution.py:195
  91.2 19.4 %collective-permute-done.10 = bf16[1,1024,1408]{2,1,0:T(8,128)(2,1)} collective-permute-done((bf16[1,1024,1408]{2,1,0:T(8,128)(2,1)}, bf16[1,1024,1408]{2,1,0:T(8,128)(2,1)}, u32[]{:S(2)}, u32[]{:S(2)}) %collective-permute-start.10) | collective-permute-done | bytes 2883616 | tf_op jit(solution)/shard_map/ppermute | solution.py:26
  110.6 8.7 %maximum_select_fusion = bf16[2048,1408]{1,0:T(8,128)(2,1)} fusion(bf16[1024,1408]{1,0:T(8,128)(2,1)} %bitcast.30, bf16[1024,1408]{1,0:T(8,128)(2,1)} %bitcast.29, pred[]{:T(512)S(6)} %eq.98), kind=kLoop, calls=%fused_computation | loop fusion | flops 25952256 | bytes 11534337 | tf_op jit(solution)/shard_map/jit(_where)/select_n | solution.py:201
  119.2 3.5 %maximum_select_fusion.1 = bf16[704,2048]{1,0:T(8,128)(2,1)S(1)} fusion(bf16[704,1024]{1,0:T(8,128)(2,1)} %bitcast.28, bf16[704,1024]{1,0:T(8,128)(2,1)} %bitcast.27, pred[]{:T(512)S(6)} %eq.98), kind=kLoop, calls=%fused_computation.7 | loop fusion | flops 12976128 | bytes 5767169 | tf_op jit(solution)/shard_map/jit(_where)/select_n | solution.py:206
  122.8 15.9 %all-to-all-done.2 = bf16[16,32,2048]{2,1,0:T(8,128)(2,1)} async-done(((bf16[16,32,2048]{2,1,0:T(8,128)(2,1)}), bf16[16,32,2048]{2,1,0:T(8,128)(2,1)}, u32[]{:S(2)}, u32[]{:S(2)}) %all-to-all-start.2) | async-done | bytes 2097184 | tf_op jit(solution)/shard_map/all_to_all | solution.py:195
  138.7 6.4 %fusion.26 = f32[512,1408]{1,0:T(8,128)S(1)} fusion(bf16[512,2048]{1,0:T(8,128)(2,1)} %bitcast.26, bf16[2048,1408]{1,0:T(8,128)(2,1)} %maximum_select_fusion), kind=kOutput, calls=%fused_computation.80 | convolution fusion | flops 2952790016 | bytes 10747904 | tf_op jit(solution)/shard_map/dot_general | solution.py:215
  145.1 3.3 %convolution_convert_fusion = bf16[512,2048]{1,0:T(8,128)(2,1)} fusion(bf16[704,2048]{1,0:T(8,128)(2,1)S(1)} %maximum_select_fusion.1, f32[512,1408]{1,0:T(8,128)S(1)} %fusion.26), kind=kOutput, calls=%fused_computation.5 | convolution fusion | flops 1479606272 | bytes 8126464 | tf_op jit(solution)/shard_map/dot_general | solution.py:217
  148.3 5.0 %all-to-all-start.3 = ((bf16[16,32,2048]{2,1,0:T(8,128)(2,1)}), bf16[16,32,2048]{2,1,0:T(8,128)(2,1)S(1)}, u32[]{:S(2)}, u32[]{:S(2)}) async-start(bf16[16,32,2048]{2,1,0:T(8,128)(2,1)} %bitcast.76), calls=%async_computation.3 | async-start | bytes 4194304 | tf_op jit(solution)/shard_map/all_to_all | solution.py:218
  153.4 0.2 select_reduce_fusion
  153.5 47.2 %all-to-all-done.3 = bf16[16,32,2048]{2,1,0:T(8,128)(2,1)S(1)} async-done(((bf16[16,32,2048]{2,1,0:T(8,128)(2,1)}), bf16[16,32,2048]{2,1,0:T(8,128)(2,1)S(1)}, u32[]{:S(2)}, u32[]{:S(2)}) %all-to-all-start.3) | async-done | bytes 2097184 | tf_op jit(solution)/shard_map/all_to_all | solution.py:218
  200.8 1.9 fusion.2
  (45 shorter events, 0.9 us)
Async XLA Ops:
  0.0 7.9 %copy-start = (s32[2,96]{1,0:T(2,128)S(1)}, s32[2,96]{1,0:T(2,128)}, u32[]{:S(2)}) copy-start(s32[2,96]{1,0:T(2,128)} %param.15) | copy-start | bytes 2308
  0.0 27.4 %copy-start.1 = (bf16[512,128]{1,0:T(8,128)(2,1)S(1)}, bf16[512,128]{1,0:T(8,128)(2,1)}, u32[]{:S(2)}) copy-start(bf16[512,128]{1,0:T(8,128)(2,1)} %param.18) | copy-start | bytes 393220
  0.0 10.8 %collective-permute-start.6 = (bf16[512,128]{1,0:T(8,128)(2,1)}, bf16[512,128]{1,0:T(8,128)(2,1)S(1)}, u32[]{:S(2)}, u32[]{:S(2)}) collective-permute-start(bf16[512,128]{1,0:T(8,128)(2,1)} %param.18), channel_id=1, source_target_pairs={{0,28},{1,29},{2,30},{3,31},{4,24},{5,25},{6,26},{7,27},{8,20},{9,... | collective-permute-start | bytes 393224 | tf_op jit(solution)/shard_map/ppermute | solution.py:87
  2.3 10.7 %collective-permute-start = (bf16[512,128]{1,0:T(8,128)(2,1)}, bf16[512,128]{1,0:T(8,128)(2,1)S(1)}, u32[]{:S(2)}, u32[]{:S(2)}) collective-permute-start(bf16[512,128]{1,0:T(8,128)(2,1)} %param.18), channel_id=1, source_target_pairs={{0,16},{1,17},{2,18},{3,19},{4,20},{5,21},{6,22},{7,23},{8,24},{9,... | collective-permute-start | bytes 393224 | tf_op jit(solution)/shard_map/ppermute | solution.py:87
  2.5 12.5 %collective-permute-start.1 = (bf16[512,128]{1,0:T(8,128)(2,1)}, bf16[512,128]{1,0:T(8,128)(2,1)S(1)}, u32[]{:S(2)}, u32[]{:S(2)}) collective-permute-start(bf16[512,128]{1,0:T(8,128)(2,1)} %param.18), channel_id=1, source_target_pairs={{0,4},{1,5},{2,6},{3,7},{4,0},{5,1},{6,2},{7,3},{8,12},{9,13},{10,... | collective-permute-start | bytes 393224 | tf_op jit(solution)/shard_map/ppermute | solution.py:85
  4.7 11.4 %collective-permute-start.2 = (bf16[512,128]{1,0:T(8,128)(2,1)}, bf16[512,128]{1,0:T(8,128)(2,1)S(1)}, u32[]{:S(2)}, u32[]{:S(2)}) collective-permute-start(bf16[512,128]{1,0:T(8,128)(2,1)} %param.18), channel_id=1, source_target_pairs={{0,20},{1,21},{2,22},{3,23},{4,16},{5,17},{6,18},{7,19},{8,28},{9,... | collective-permute-start | bytes 393224 | tf_op jit(solution)/shard_map/ppermute | solution.py:87
  5.6 10.8 %collective-permute-start.3 = (bf16[512,128]{1,0:T(8,128)(2,1)}, bf16[512,128]{1,0:T(8,128)(2,1)S(1)}, u32[]{:S(2)}, u32[]{:S(2)}) collective-permute-start(bf16[512,128]{1,0:T(8,128)(2,1)} %param.18), channel_id=1, source_target_pairs={{0,8},{1,9},{2,10},{3,11},{4,12},{5,13},{6,14},{7,15},{8,0},{9,1},... | collective-permute-start | bytes 393224 | tf_op jit(solution)/shard_map/ppermute | solution.py:85
  10.8 13.0 %collective-permute-start.4 = (bf16[512,128]{1,0:T(8,128)(2,1)}, bf16[512,128]{1,0:T(8,128)(2,1)S(1)}, u32[]{:S(2)}, u32[]{:S(2)}) collective-permute-start(bf16[512,128]{1,0:T(8,128)(2,1)} %param.18), channel_id=1, source_target_pairs={{0,24},{1,25},{2,26},{3,27},{4,28},{5,29},{6,30},{7,31},{8,16},{9,... | collective-permute-start | bytes 393224 | tf_op jit(solution)/shard_map/ppermute | solution.py:87
  13.0 14.5 %collective-permute-start.5 = (bf16[512,128]{1,0:T(8,128)(2,1)}, bf16[512,128]{1,0:T(8,128)(2,1)S(1)}, u32[]{:S(2)}, u32[]{:S(2)}) collective-permute-start(bf16[512,128]{1,0:T(8,128)(2,1)} %param.18), channel_id=1, source_target_pairs={{0,12},{1,13},{2,14},{3,15},{4,8},{5,9},{6,10},{7,11},{8,4},{9,5},... | collective-permute-start | bytes 393224 | tf_op jit(solution)/shard_map/ppermute | solution.py:85
  15.0 67.0 %collective-permute-start.9 = (bf16[1,704,1024]{2,1,0:T(8,128)(2,1)}, bf16[1,704,1024]{2,1,0:T(8,128)(2,1)}, u32[]{:S(2)}, u32[]{:S(2)}) collective-permute-start(bf16[1,704,1024]{2,1,0:T(8,128)(2,1)} %param.23), channel_id=1, source_target_pairs={{0,16},{16,0},{1,17},{17,1},{2,18},{18,2},{3,19},{19,3},{4,20},{20... | collective-permute-start | bytes 4325384 | tf_op jit(solution)/shard_map/ppermute | solution.py:26
  16.1 94.5 %collective-permute-start.10 = (bf16[1,1024,1408]{2,1,0:T(8,128)(2,1)}, bf16[1,1024,1408]{2,1,0:T(8,128)(2,1)}, u32[]{:S(2)}, u32[]{:S(2)}) collective-permute-start(bf16[1,1024,1408]{2,1,0:T(8,128)(2,1)} %param.22), channel_id=1, source_target_pairs={{0,16},{16,0},{1,17},{17,1},{2,18},{18,2},{3,19},{19,3},{4,20},{20... | collective-permute-start | bytes 8650760 | tf_op jit(solution)/shard_map/ppermute | solution.py:26
  27.7 1.5 copy-start.6
  28.3 7.6 %copy-start.7 = (s32[1,16]{1,0:T(1,128)S(1)}, s32[1,16]{1,0:T(1,128)}, u32[]{:S(2)}) copy-start(s32[1,16]{1,0:T(1,128)} %param.17) | copy-start | bytes 196
  28.8 31.9 %collective-permute-start.7 = (bf16[4,1024,128]{2,1,0:T(8,128)(2,1)S(1)}, bf16[4,1024,128]{2,1,0:T(8,128)(2,1)S(1)}, u32[]{:S(2)}, u32[]{:S(2)}) collective-permute-start(bf16[4,1024,128]{2,1,0:T(8,128)(2,1)S(1)} %pad_maximum_fusion.1), channel_id=1, source_target_pairs={{0,2},{1,3},{2,0},{3,1},{4,6},{5,7},{6,4},{7,5},{8,10},{9,11},{10,... | collective-permute-start | bytes 3145736 | tf_op jit(solution)/shard_map/ppermute | solution.py:149
  29.9 33.5 %all-to-all-start = ((bf16[16,224,128]{2,1,0:T(8,128)(2,1)}), bf16[16,224,128]{2,1,0:T(8,128)(2,1)S(1)}, u32[]{:S(2)}, u32[]{:S(2)}) async-start(bf16[16,224,128]{2,1,0:T(8,128)(2,1)} %pad_maximum_fusion.2), calls=%async_computation | async-start | bytes 1835008 | tf_op jit(solution)/shard_map/all_to_all | solution.py:124
  61.0 17.6 %collective-permute-start.8 = (bf16[8,1024,128]{2,1,0:T(8,128)(2,1)S(1)}, bf16[8,1024,128]{2,1,0:T(8,128)(2,1)}, u32[]{:S(2)}, u32[]{:S(2)}) collective-permute-start(bf16[8,1024,128]{2,1,0:T(8,128)(2,1)S(1)} %pad_maximum_fusion), channel_id=1, source_target_pairs={{0,1},{1,0},{2,3},{3,2},{4,5},{5,4},{6,7},{7,6},{8,9},{9,8},{10,11... | collective-permute-start | bytes 6291464 | tf_op jit(solution)/shard_map/ppermute | solution.py:154
  65.7 7.1 %copy-start.3 = (s32[64,6]{0,1:T(8,128)S(1)}, s32[64,6]{0,1:T(8,128)}, u32[]{:S(2)}) copy-start(s32[64,6]{0,1:T(8,128)} %param.20) | copy-start | bytes 4612
  67.1 10.9 %all-to-all-start.1 = ((bf16[16,32,128]{2,1,0:T(8,128)(2,1)}), bf16[16,32,128]{2,1,0:T(8,128)(2,1)S(1)}, u32[]{:S(2)}, u32[]{:S(2)}) async-start(bf16[16,32,128]{2,1,0:T(8,128)(2,1)} %bitcast.19), calls=%async_computation.1 | async-start | bytes 262144 | tf_op jit(solution)/shard_map/all_to_all | solution.py:142
  78.6 3.0 %copy-start.2 = (bf16[64,2048]{1,0:T(8,128)(2,1)S(1)}, bf16[64,2048]{1,0:T(8,128)(2,1)}, u32[]{:S(2)}) copy-start(bf16[64,2048]{1,0:T(8,128)(2,1)} %param.13) | copy-start | bytes 786436
  78.6 3.2 %copy-start.4 = (f32[2048]{0:T(1024)S(1)}, f32[2048]{0:T(1024)}, u32[]{:S(2)}) copy-start(f32[2048]{0:T(1024)} %param.19) | copy-start | bytes 24580
  84.1 54.6 %all-to-all-start.2 = ((bf16[16,32,2048]{2,1,0:T(8,128)(2,1)}), bf16[16,32,2048]{2,1,0:T(8,128)(2,1)}, u32[]{:S(2)}, u32[]{:S(2)}) async-start(bf16[16,32,2048]{2,1,0:T(8,128)(2,1)} %bitcast.25), calls=%async_computation.2 | async-start | bytes 4194304 | tf_op jit(solution)/shard_map/all_to_all | solution.py:195
  148.3 5.0 %copy-start.5 = (f32[64,6]{0,1:T(8,128)S(1)}, f32[64,6]{0,1:T(8,128)}, u32[]{:S(2)}) copy-start(f32[64,6]{0,1:T(8,128)} %param.21) | copy-start | bytes 4612
  148.3 52.4 %all-to-all-start.3 = ((bf16[16,32,2048]{2,1,0:T(8,128)(2,1)}), bf16[16,32,2048]{2,1,0:T(8,128)(2,1)S(1)}, u32[]{:S(2)}, u32[]{:S(2)}) async-start(bf16[16,32,2048]{2,1,0:T(8,128)(2,1)} %bitcast.76), calls=%async_computation.3 | async-start | bytes 4194304 | tf_op jit(solution)/shard_map/all_to_all | solution.py:218
where the time goes:
time: 203 us
  waiting for transfers between devices  122 us (60%)
  starting transfers between devices  36.1 us (18%)
  matrix products  18.3 us (9%)
  other arithmetic  18 us (9%)
  local copies, waits for them, and re-layouts  7.32 us (4%)
    all_to_all x1, waiting for transfers between devices, on_device(): lax.all_to_all(outcome.reshape(n_mp, capacity, d_model), 'mp', split_axis...  47.2 us
    ppermute x1, waiting for transfers between devices, on_device(): pair = lax.ppermute(block, 'mp', [(m, m ^ 1 << b) for m in range(n_mp)])  23.9 us
    ppermute x2, waiting for transfers between devices, swap_dp(): return lax.ppermute(x, 'dp', [(0, 1), (1, 0)])  19.4 us
    all_to_all x1, waiting for transfers between devices, on_device(): lax.all_to_all(sending.reshape(n_mp, capacity, d_model), 'mp', split_axis...  15.9 us
    select_n x1, other arithmetic, on_device(): jnp.where(first, jnp.concatenate([experts_in[0], in_other[0]], axis=0), j...  8.66 us
    ppermute x4, waiting for transfers between devices, on_device(): lax.ppermute(out_weight, ('dp', 'mp'), [(d * n_mp + m, (1 - d) * n_mp + (...  7.35 us
    all_to_all x1, starting transfers between devices, on_device(): lax.all_to_all(sending.reshape(n_mp, capacity, d_model), 'mp', split_axis...  7.07 us
    dot_general x1, matrix products, on_device(): gate_vals = jnp.dot(flat_rows, gate_up, preferred_element_type=jnp.float32)  6.38 us
  transfers between devices with their start and end apart: 15, of which 7 were waited for; matrix products, arithmetic and copies ran while one was open for 16% of the time, Pallas kernels for 0%

commit v1 on v0

--- a/solution.py
+++ b/solution.py
@@ -192,9 +192,19 @@
     sending = lax.dot_general(
         dispatch, normed, (((0,), (0,)), ((), ())), preferred_element_type=jnp.float32
     ).astype(jnp.bfloat16)
-    received = lax.all_to_all(
-        sending.reshape(n_mp, capacity, d_model), "mp", split_axis=0, concat_axis=0, tiled=True
-    )
+    shard = sending.reshape(n_mp, capacity, d_model)
+    ways, here = (lax.axis_size("mp"), lax.axis_index("mp"))
+    width_2 = shard.shape[0] // ways
+    shape = list(shard.shape)
+    shape[0] = width_2
+    height = shape[0]
+    shape[0] = height * ways
+    received = jnp.zeros(shape, shard.dtype)
+    for mask in range(ways):
+        part = lax.dynamic_slice_in_dim(shard, (here ^ mask) * width_2, width_2, axis=0)
+        if mask:
+            part = lax.ppermute(part, "mp", [(d_2, d_2 ^ mask) for d_2 in range(ways)])
+        received = lax.dynamic_update_slice_in_dim(received, part, (here ^ mask) * height, axis=0)
     flat_rows = received.reshape(-1, d_model)
     if n_dp == 2:
         first = row_index == 0

time: 203 us -> 250 us (1.23)
  waiting for transfers between devices: 122 us -> 160 us
  starting transfers between devices: 36.1 us -> 46.5 us
  matrix products: 18.3 us -> 14 us
    ppermute x0 -> x15, waiting for transfers between devices: none -> 39.4 us  [on_device(): part = lax.ppermute(part, 'mp', [(d_2, d_2 ^ mask) for d_2 in range(ways)])]
    ppermute x0 -> x15, starting transfers between devices: none -> 17.2 us  [on_device(): part = lax.ppermute(part, 'mp', [(d_2, d_2 ^ mask) for d_2 in range(ways)])]
    all_to_all x1 -> x0, waiting for transfers between devices: 15.9 us -> none  [on_device(): lax.all_to_all(sending.reshape(n_mp, capacity, d_model), 'mp', split_axis...]
    ppermute x2, waiting for transfers between devices: 19.4 us -> 27.2 us  [swap_dp(): return lax.ppermute(x, 'dp', [(0, 1), (1, 0)])]
    ppermute x1, waiting for transfers between devices: 23.9 us -> 31.5 us  [on_device(): pair = lax.ppermute(block, 'mp', [(m, m ^ 1 << b) for m in range(n_mp)])]
    all_to_all x1 -> x0, starting transfers between devices: 7.07 us -> none  [on_device(): lax.all_to_all(sending.reshape(n_mp, capacity, d_model), 'mp', split_axis...]
    dot_general x1, matrix products: 6.38 us -> 3.42 us  [on_device(): gate_vals = jnp.dot(flat_rows, gate_up, preferred_element_type=jnp.float32)]
  transfers between devices with their start and end apart: 15 -> 29, of which waited for: 7 -> 15; matrix products, arithmetic and copies ran while one was open for 16% -> 13% of each run, Pallas kernels for 0% -> 0%
where the time goes in v1:
time: 250 us; the launch traced here: 249 us
  waiting for transfers between devices  160 us (64%)
  starting transfers between devices  46.5 us (19%)
  other arithmetic  19.1 us (8%)
  matrix products  14 us (6%)
  local copies, waits for them, and re-layouts  8.61 us (3%)
    all_to_all x1, waiting for transfers between devices, on_device(): lax.all_to_all(outcome.reshape(n_mp, capacity, d_model), 'mp', split_axis...  47.2 us
    ppermute x15, waiting for transfers between devices, on_device(): part = lax.ppermute(part, 'mp', [(d_2, d_2 ^ mask) for d_2 in range(ways)])  39.4 us
    ppermute x1, waiting for transfers between devices, on_device(): pair = lax.ppermute(block, 'mp', [(m, m ^ 1 << b) for m in range(n_mp)])  31.5 us
    ppermute x2, waiting for transfers between devices, swap_dp(): return lax.ppermute(x, 'dp', [(0, 1), (1, 0)])  27.2 us
    ppermute x15, starting transfers between devices, on_device(): part = lax.ppermute(part, 'mp', [(d_2, d_2 ^ mask) for d_2 in range(ways)])  17.2 us
    select_n x1, other arithmetic, on_device(): jnp.where(first, jnp.concatenate([experts_in[0], in_other[0]], axis=0), j...  8.75 us
    ppermute x4, waiting for transfers between devices, on_device(): lax.ppermute(out_weight, ('dp', 'mp'), [(d * n_mp + m, (1 - d) * n_mp + (...  6.53 us
    all_to_all x1, starting transfers between devices, on_device(): lax.all_to_all(kv_send, 'mp', split_axis=0, concat_axis=0, tiled=True)  6.28 us
  transfers between devices with their start and end apart: 29, of which 15 were waited for; matrix products, arithmetic and copies ran while one was open for 13% of the time, Pallas kernels for 0%

profile of v1, /device:TPU:11, one launch (start us, length us, event | category | flops | bytes accessed | tf_op | source)
XLA Modules:
  0.0 248.5 jit_solution(13510298858584634974)
XLA Ops:
  0.0 2.3 collective-permute-start.6
  2.5 2.2 collective-permute-start.1
  4.7 1.0 collective-permute-start.2
  5.9 1.2 dynamic_slice.55
  7.1 1.3 fusion.19
  8.5 0.8 copy.72
  9.7 1.2 reshape.608
  10.9 0.3 copy.66
  11.2 0.9 copy.77
  12.3 2.2 collective-permute-start.4
  14.5 0.4 collective-permute-start.5
  14.9 0.6 tile.8
  15.5 1.0 pad_maximum_fusion.2
  16.5 1.1 collective-permute-start.9
  17.6 0.4 collective-permute-start.25
  18.0 6.5 %collective-permute-done.4 = bf16[512,128]{1,0:T(8,128)(2,1)S(1)} collective-permute-done((bf16[512,128]{1,0:T(8,128)(2,1)S(1)}, bf16[512,128]{1,0:T(8,128)(2,1)S(1)}, u32[]{:S(2)}, u32[]{:S(2)}) %collective-permute-start.4) | collective-permute-done | bytes 131104 | tf_op jit(solution)/shard_map/ppermute | solution.py:87
  24.5 2.8 %collective-permute-done.5 = bf16[512,128]{1,0:T(8,128)(2,1)S(1)} collective-permute-done((bf16[512,128]{1,0:T(8,128)(2,1)S(1)}, bf16[512,128]{1,0:T(8,128)(2,1)S(1)}, u32[]{:S(2)}, u32[]{:S(2)}) %collective-permute-start.5) | collective-permute-done | bytes 131104 | tf_op jit(solution)/shard_map/ppermute | solution.py:85
  27.3 0.3 broadcast_select_fusion.4
  27.6 0.3 broadcast_select_fusion.5
  27.9 0.3 broadcast_select_fusion.8
  28.2 0.3 broadcast_select_fusion.9
  28.6 6.3 %all-to-all-start = ((bf16[16,224,128]{2,1,0:T(8,128)(2,1)}), bf16[16,224,128]{2,1,0:T(8,128)(2,1)S(1)}, u32[]{:S(2)}, u32[]{:S(2)}) async-start(bf16[16,224,128]{2,1,0:T(8,128)(2,1)} %pad_maximum_fusion.2), calls=%async_computation | async-start | bytes 1835008 | tf_op jit(solution)/shard_map/all_to_all | solution.py:124
  35.0 0.3 collective-permute-start.7
  35.6 0.9 reduce-window.6
  37.0 31.5 %collective-permute-done.7 = bf16[4,1024,128]{2,1,0:T(8,128)(2,1)S(1)} collective-permute-done((bf16[4,1024,128]{2,1,0:T(8,128)(2,1)S(1)}, bf16[4,1024,128]{2,1,0:T(8,128)(2,1)S(1)}, u32[]{:S(2)}, u32[]{:S(2)}) %collective-permute-start.7) | collective-permute-done | bytes 1048608 | tf_op jit(solution)/shard_map/ppermute | solution.py:149
  68.9 0.8 collective-permute-start.8
  69.8 0.5 copy.67
  70.6 0.7 fusion.24
  71.3 0.6 fusion.1
  72.0 1.4 fusion.5
  73.4 5.8 %all-to-all-start.1 = ((bf16[16,32,128]{2,1,0:T(8,128)(2,1)}), bf16[16,32,128]{2,1,0:T(8,128)(2,1)S(1)}, u32[]{:S(2)}, u32[]{:S(2)}) async-start(bf16[16,32,128]{2,1,0:T(8,128)(2,1)} %bitcast.19), calls=%async_computation.1 | async-start | bytes 262144 | tf_op jit(solution)/shard_map/all_to_all | solution.py:142
  79.3 5.0 %all-to-all-done.1 = bf16[16,32,128]{2,1,0:T(8,128)(2,1)S(1)} async-done(((bf16[16,32,128]{2,1,0:T(8,128)(2,1)}), bf16[16,32,128]{2,1,0:T(8,128)(2,1)S(1)}, u32[]{:S(2)}, u32[]{:S(2)}) %all-to-all-start.1) | async-done | bytes 131104 | tf_op jit(solution)/shard_map/all_to_all | solution.py:142
  84.4 0.5 fusion.25
  84.9 27.2 %collective-permute-done.25 = bf16[1,1024,1408]{2,1,0:T(8,128)(2,1)} collective-permute-done((bf16[1,1024,1408]{2,1,0:T(8,128)(2,1)}, bf16[1,1024,1408]{2,1,0:T(8,128)(2,1)}, u32[]{:S(2)}, u32[]{:S(2)}) %collective-permute-start.25) | collective-permute-done | bytes 2883616 | tf_op jit(solution)/shard_map/ppermute | solution.py:26
  112.1 8.7 %maximum_select_fusion = bf16[2048,1408]{1,0:T(8,128)(2,1)} fusion(bf16[1024,1408]{1,0:T(8,128)(2,1)} %bitcast.30, bf16[1024,1408]{1,0:T(8,128)(2,1)} %bitcast.29, pred[]{:T(512)S(6)} %eq.98), kind=kLoop, calls=%fused_computation | loop fusion | flops 25952256 | bytes 11534337 | tf_op jit(solution)/shard_map/jit(_where)/select_n | solution.py:211
  120.9 2.1 fusion.26
  123.0 0.4 copy.71
  123.4 0.4 reshape.614
  124.3 0.8 convolution_convert_fusion.1
  125.5 1.9 collective-permute-start.10
  127.7 1.4 collective-permute-start.12
  129.2 1.5 collective-permute-start.13
  130.6 0.3 collective-permute-start.14
  131.0 3.9 %maximum_select_fusion.1 = bf16[704,2048]{1,0:T(8,128)(2,1)S(1)} fusion(bf16[704,1024]{1,0:T(8,128)(2,1)} %bitcast.28, bf16[704,1024]{1,0:T(8,128)(2,1)} %bitcast.27, pred[]{:T(512)S(6)} %eq.98), kind=kLoop, calls=%fused_computation.7 | loop fusion | flops 12976128 | bytes 5767169 | tf_op jit(solution)/shard_map/jit(_where)/select_n | solution.py:216
  134.9 1.5 collective-permute-start.15
  136.4 1.3 collective-permute-start.16
  137.8 3.4 %collective-permute-start.17 = (bf16[1,32,2048]{2,1,0:T(8,128)(2,1)S(1)}, bf16[1,32,2048]{2,1,0:T(8,128)(2,1)S(1)}, u32[]{:S(2)}, u32[]{:S(2)}) collective-permute-start(bf16[1,32,2048]{2,1,0:T(8,128)(2,1)S(1)} %get-tuple-element.28), channel_id=1, source_target_pairs={{0,8},{1,9},{2,10},{3,11},{4,12},{5,13},{6,14},{7,15},{8,0},{9,1},... | collective-permute-start | bytes 393224 | tf_op jit(solution)/shard_map/ppermute | solution.py:206
  141.4 2.7 %collective-permute-start.19 = (bf16[1,32,2048]{2,1,0:T(8,128)(2,1)S(1)}, bf16[1,32,2048]{2,1,0:T(8,128)(2,1)S(1)}, u32[]{:S(2)}, u32[]{:S(2)}) collective-permute-start(bf16[1,32,2048]{2,1,0:T(8,128)(2,1)S(1)} %get-tuple-element.26), channel_id=1, source_target_pairs={{0,10},{1,11},{2,8},{3,9},{4,14},{5,15},{6,12},{7,13},{8,2},{9,3},... | collective-permute-start | bytes 393224 | tf_op jit(solution)/shard_map/ppermute | solution.py:206
  144.1 1.4 collective-permute-start.20
  145.6 0.3 collective-permute-done.16
  145.8 1.2 collective-permute-start.21
  147.0 11.1 %collective-permute-done.17 = bf16[1,32,2048]{2,1,0:T(8,128)(2,1)S(1)} collective-permute-done((bf16[1,32,2048]{2,1,0:T(8,128)(2,1)S(1)}, bf16[1,32,2048]{2,1,0:T(8,128)(2,1)S(1)}, u32[]{:S(2)}, u32[]{:S(2)}) %collective-permute-start.17) | collective-permute-done | bytes 131104 | tf_op jit(solution)/shard_map/ppermute | solution.py:206
  158.1 2.8 %collective-permute-done.18 = bf16[1,32,2048]{2,1,0:T(8,128)(2,1)S(1)} collective-permute-done((bf16[1,32,2048]{2,1,0:T(8,128)(2,1)S(1)}, bf16[1,32,2048]{2,1,0:T(8,128)(2,1)S(1)}, u32[]{:S(2)}, u32[]{:S(2)}) %collective-permute-start.18) | collective-permute-done | bytes 131104 | tf_op jit(solution)/shard_map/ppermute | solution.py:206
  161.0 8.2 %collective-permute-done.19 = bf16[1,32,2048]{2,1,0:T(8,128)(2,1)S(1)} collective-permute-done((bf16[1,32,2048]{2,1,0:T(8,128)(2,1)S(1)}, bf16[1,32,2048]{2,1,0:T(8,128)(2,1)S(1)}, u32[]{:S(2)}, u32[]{:S(2)}) %collective-permute-start.19) | collective-permute-done | bytes 131104 | tf_op jit(solution)/shard_map/ppermute | solution.py:206
  169.2 2.9 %collective-permute-done.20 = bf16[1,32,2048]{2,1,0:T(8,128)(2,1)S(1)} collective-permute-done((bf16[1,32,2048]{2,1,0:T(8,128)(2,1)S(1)}, bf16[1,32,2048]{2,1,0:T(8,128)(2,1)S(1)}, u32[]{:S(2)}, u32[]{:S(2)}) %collective-permute-start.20) | collective-permute-done | bytes 131104 | tf_op jit(solution)/shard_map/ppermute | solution.py:206
  172.2 2.8 %collective-permute-done.21 = bf16[1,32,2048]{2,1,0:T(8,128)(2,1)S(1)} collective-permute-done((bf16[1,32,2048]{2,1,0:T(8,128)(2,1)S(1)}, bf16[1,32,2048]{2,1,0:T(8,128)(2,1)S(1)}, u32[]{:S(2)}, u32[]{:S(2)}) %collective-permute-start.21) | collective-permute-done | bytes 131104 | tf_op jit(solution)/shard_map/ppermute | solution.py:206
  175.0 6.6 %collective-permute-done.22 = bf16[1,32,2048]{2,1,0:T(8,128)(2,1)S(1)} collective-permute-done((bf16[1,32,2048]{2,1,0:T(8,128)(2,1)S(1)}, bf16[1,32,2048]{2,1,0:T(8,128)(2,1)S(1)}, u32[]{:S(2)}, u32[]{:S(2)}) %collective-permute-start.22) | collective-permute-done | bytes 131104 | tf_op jit(solution)/shard_map/ppermute | solution.py:206
  181.6 1.9 collective-permute-done.23
  183.5 2.8 %collective-permute-done.24 = bf16[1,32,2048]{2,1,0:T(8,128)(2,1)S(1)} collective-permute-done((bf16[1,32,2048]{2,1,0:T(8,128)(2,1)S(1)}, bf16[1,32,2048]{2,1,0:T(8,128)(2,1)S(1)}, u32[]{:S(2)}, u32[]{:S(2)}) %collective-permute-start.24) | collective-permute-done | bytes 131104 | tf_op jit(solution)/shard_map/ppermute | solution.py:206
  186.3 3.4 %fusion.27 = f32[512,1408]{1,0:T(8,128)S(1)} fusion(bf16[512,2048]{1,0:T(8,128)(2,1)S(1)} %bitcast.79, bf16[2048,1408]{1,0:T(8,128)(2,1)S(1)} %bitcast.76), kind=kOutput, calls=%fused_computation.112 | convolution fusion | flops 2952790016 | bytes 10747904 | tf_op jit(solution)/shard_map/dot_general | solution.py:225
  189.8 3.2 %convolution_convert_fusion = bf16[512,2048]{1,0:T(8,128)(2,1)} fusion(bf16[704,2048]{1,0:T(8,128)(2,1)S(1)} %maximum_select_fusion.1, f32[512,1408]{1,0:T(8,128)S(1)} %fusion.27), kind=kOutput, calls=%fused_computation.5 | convolution fusion | flops 1479606272 | bytes 8126464 | tf_op jit(solution)/shard_map/dot_general | solution.py:227
  193.0 6.2 %all-to-all-start.2 = ((bf16[16,32,2048]{2,1,0:T(8,128)(2,1)}), bf16[16,32,2048]{2,1,0:T(8,128)(2,1)S(1)}, u32[]{:S(2)}, u32[]{:S(2)}) async-start(bf16[16,32,2048]{2,1,0:T(8,128)(2,1)} %bitcast.80), calls=%async_computation.2 | async-start | bytes 4194304 | tf_op jit(solution)/shard_map/all_to_all | solution.py:228
  199.4 47.2 %all-to-all-done.2 = bf16[16,32,2048]{2,1,0:T(8,128)(2,1)S(1)} async-done(((bf16[16,32,2048]{2,1,0:T(8,128)(2,1)}), bf16[16,32,2048]{2,1,0:T(8,128)(2,1)S(1)}, u32[]{:S(2)}, u32[]{:S(2)}) %all-to-all-start.2) | async-done | bytes 2097184 | tf_op jit(solution)/shard_map/all_to_all | solution.py:228
  246.6 1.9 fusion.2
  (91 shorter events, 4.8 us)
Async XLA Ops:
  0.0 8.5 %copy-start = (s32[2,96]{1,0:T(2,128)S(1)}, s32[2,96]{1,0:T(2,128)}, u32[]{:S(2)}) copy-start(s32[2,96]{1,0:T(2,128)} %param.15) | copy-start | bytes 2308
  0.0 12.3 %copy-start.1 = (bf16[512,128]{1,0:T(8,128)(2,1)S(1)}, bf16[512,128]{1,0:T(8,128)(2,1)}, u32[]{:S(2)}) copy-start(bf16[512,128]{1,0:T(8,128)(2,1)} %param.18) | copy-start | bytes 393220
  0.0 12.3 %collective-permute-start.6 = (bf16[512,128]{1,0:T(8,128)(2,1)}, bf16[512,128]{1,0:T(8,128)(2,1)S(1)}, u32[]{:S(2)}, u32[]{:S(2)}) collective-permute-start(bf16[512,128]{1,0:T(8,128)(2,1)} %param.18), channel_id=1, source_target_pairs={{0,28},{1,29},{2,30},{3,31},{4,24},{5,25},{6,26},{7,27},{8,20},{9,... | collective-permute-start | bytes 393224 | tf_op jit(solution)/shard_map/ppermute | solution.py:87
  2.3 12.3 %collective-permute-start = (bf16[512,128]{1,0:T(8,128)(2,1)}, bf16[512,128]{1,0:T(8,128)(2,1)S(1)}, u32[]{:S(2)}, u32[]{:S(2)}) collective-permute-start(bf16[512,128]{1,0:T(8,128)(2,1)} %param.18), channel_id=1, source_target_pairs={{0,16},{1,17},{2,18},{3,19},{4,20},{5,21},{6,22},{7,23},{8,24},{9,... | collective-permute-start | bytes 393224 | tf_op jit(solution)/shard_map/ppermute | solution.py:87
  2.5 14.0 %collective-permute-start.1 = (bf16[512,128]{1,0:T(8,128)(2,1)}, bf16[512,128]{1,0:T(8,128)(2,1)S(1)}, u32[]{:S(2)}, u32[]{:S(2)}) collective-permute-start(bf16[512,128]{1,0:T(8,128)(2,1)} %param.18), channel_id=1, source_target_pairs={{0,4},{1,5},{2,6},{3,7},{4,0},{5,1},{6,2},{7,3},{8,12},{9,13},{10,... | collective-permute-start | bytes 393224 | tf_op jit(solution)/shard_map/ppermute | solution.py:85
  4.7 12.9 %collective-permute-start.2 = (bf16[512,128]{1,0:T(8,128)(2,1)}, bf16[512,128]{1,0:T(8,128)(2,1)S(1)}, u32[]{:S(2)}, u32[]{:S(2)}) collective-permute-start(bf16[512,128]{1,0:T(8,128)(2,1)} %param.18), channel_id=1, source_target_pairs={{0,20},{1,21},{2,22},{3,23},{4,16},{5,17},{6,18},{7,19},{8,28},{9,... | collective-permute-start | bytes 393224 | tf_op jit(solution)/shard_map/ppermute | solution.py:87
  5.6 12.3 %collective-permute-start.3 = (bf16[512,128]{1,0:T(8,128)(2,1)}, bf16[512,128]{1,0:T(8,128)(2,1)S(1)}, u32[]{:S(2)}, u32[]{:S(2)}) collective-permute-start(bf16[512,128]{1,0:T(8,128)(2,1)} %param.18), channel_id=1, source_target_pairs={{0,8},{1,9},{2,10},{3,11},{4,12},{5,13},{6,14},{7,15},{8,0},{9,1},... | collective-permute-start | bytes 393224 | tf_op jit(solution)/shard_map/ppermute | solution.py:85
  12.3 12.2 %collective-permute-start.4 = (bf16[512,128]{1,0:T(8,128)(2,1)S(1)}, bf16[512,128]{1,0:T(8,128)(2,1)S(1)}, u32[]{:S(2)}, u32[]{:S(2)}) collective-permute-start(bf16[512,128]{1,0:T(8,128)(2,1)S(1)} %copy-done.1), channel_id=1, source_target_pairs={{0,24},{1,25},{2,26},{3,27},{4,28},{5,29},{6,30},{7,31},{8,16},{9,... | collective-permute-start | bytes 393224 | tf_op jit(solution)/shard_map/ppermute | solution.py:87
  14.5 12.8 %collective-permute-start.5 = (bf16[512,128]{1,0:T(8,128)(2,1)S(1)}, bf16[512,128]{1,0:T(8,128)(2,1)S(1)}, u32[]{:S(2)}, u32[]{:S(2)}) collective-permute-start(bf16[512,128]{1,0:T(8,128)(2,1)S(1)} %copy-done.1), channel_id=1, source_target_pairs={{0,12},{1,13},{2,14},{3,15},{4,8},{5,9},{6,10},{7,11},{8,4},{9,5},... | collective-permute-start | bytes 393224 | tf_op jit(solution)/shard_map/ppermute | solution.py:85
  16.5 107.8 %collective-permute-start.9 = (bf16[1,704,1024]{2,1,0:T(8,128)(2,1)}, bf16[1,704,1024]{2,1,0:T(8,128)(2,1)}, u32[]{:S(2)}, u32[]{:S(2)}) collective-permute-start(bf16[1,704,1024]{2,1,0:T(8,128)(2,1)} %param.23), channel_id=1, source_target_pairs={{0,16},{16,0},{1,17},{17,1},{2,18},{18,2},{3,19},{19,3},{4,20},{20... | collective-permute-start | bytes 4325384 | tf_op jit(solution)/shard_map/ppermute | solution.py:26
  17.6 94.5 %collective-permute-start.25 = (bf16[1,1024,1408]{2,1,0:T(8,128)(2,1)}, bf16[1,1024,1408]{2,1,0:T(8,128)(2,1)}, u32[]{:S(2)}, u32[]{:S(2)}) collective-permute-start(bf16[1,1024,1408]{2,1,0:T(8,128)(2,1)} %param.22), channel_id=1, source_target_pairs={{0,16},{16,0},{1,17},{17,1},{2,18},{18,2},{3,19},{19,3},{4,20},{20... | collective-permute-start | bytes 8650760 | tf_op jit(solution)/shard_map/ppermute | solution.py:26
  28.6 41.1 %all-to-all-start = ((bf16[16,224,128]{2,1,0:T(8,128)(2,1)}), bf16[16,224,128]{2,1,0:T(8,128)(2,1)S(1)}, u32[]{:S(2)}, u32[]{:S(2)}) async-start(bf16[16,224,128]{2,1,0:T(8,128)(2,1)} %pad_maximum_fusion.2), calls=%async_computation | async-start | bytes 1835008 | tf_op jit(solution)/shard_map/all_to_all | solution.py:124
  35.0 33.5 %collective-permute-start.7 = (bf16[4,1024,128]{2,1,0:T(8,128)(2,1)S(1)}, bf16[4,1024,128]{2,1,0:T(8,128)(2,1)S(1)}, u32[]{:S(2)}, u32[]{:S(2)}) collective-permute-start(bf16[4,1024,128]{2,1,0:T(8,128)(2,1)S(1)} %pad_maximum_fusion.1), channel_id=1, source_target_pairs={{0,2},{1,3},{2,0},{3,1},{4,6},{5,7},{6,4},{7,5},{8,10},{9,11},{10,... | collective-permute-start | bytes 3145736 | tf_op jit(solution)/shard_map/ppermute | solution.py:149
  68.9 52.0 %collective-permute-start.8 = (bf16[8,1024,128]{2,1,0:T(8,128)(2,1)S(1)}, bf16[8,1024,128]{2,1,0:T(8,128)(2,1)}, u32[]{:S(2)}, u32[]{:S(2)}) collective-permute-start(bf16[8,1024,128]{2,1,0:T(8,128)(2,1)S(1)} %pad_maximum_fusion), channel_id=1, source_target_pairs={{0,1},{1,0},{2,3},{3,2},{4,5},{5,4},{6,7},{7,6},{8,9},{9,8},{10,11... | collective-permute-start | bytes 6291464 | tf_op jit(solution)/shard_map/ppermute | solution.py:154
  72.0 7.2 %copy-start.3 = (s32[64,6]{0,1:T(8,128)S(1)}, s32[64,6]{0,1:T(8,128)}, u32[]{:S(2)}) copy-start(s32[64,6]{0,1:T(8,128)} %param.20) | copy-start | bytes 4612
  73.4 10.9 %all-to-all-start.1 = ((bf16[16,32,128]{2,1,0:T(8,128)(2,1)}), bf16[16,32,128]{2,1,0:T(8,128)(2,1)S(1)}, u32[]{:S(2)}, u32[]{:S(2)}) async-start(bf16[16,32,128]{2,1,0:T(8,128)(2,1)} %bitcast.19), calls=%async_computation.1 | async-start | bytes 262144 | tf_op jit(solution)/shard_map/all_to_all | solution.py:142
  123.0 1.0 copy-start.2
  123.0 1.1 copy-start.4
  125.3 61.1 %slice-start = ((s8[5767168]{0:T(1024)(128)(4,1)}), s8[4194304]{0:T(1024)(128)(4,1)S(1)}, s32[]{:S(2)}) async-start(s8[5767168]{0:T(1024)(128)(4,1)} %bitcast.75), calls=%async_computation.3 | async-start | bytes 8388608
  125.5 9.4 %collective-permute-start.10 = (bf16[1,32,2048]{2,1,0:T(8,128)(2,1)S(1)}, bf16[1,32,2048]{2,1,0:T(8,128)(2,1)S(1)}, u32[]{:S(2)}, u32[]{:S(2)}) collective-permute-start(bf16[1,32,2048]{2,1,0:T(8,128)(2,1)S(1)} %get-tuple-element.35), channel_id=1, source_target_pairs={{0,1},{1,0},{2,3},{3,2},{4,5},{5,4},{6,7},{7,6},{8,9},{9,8},{10,11... | collective-permute-start | bytes 393224 | tf_op jit(solution)/shard_map/ppermute | solution.py:206
  127.5 9.0 %collective-permute-start.11 = (bf16[1,32,2048]{2,1,0:T(8,128)(2,1)S(1)}, bf16[1,32,2048]{2,1,0:T(8,128)(2,1)S(1)}, u32[]{:S(2)}, u32[]{:S(2)}) collective-permute-start(bf16[1,32,2048]{2,1,0:T(8,128)(2,1)S(1)} %get-tuple-element.34), channel_id=1, source_target_pairs={{0,2},{1,3},{2,0},{3,1},{4,6},{5,7},{6,4},{7,5},{8,10},{9,11},{10,... | collective-permute-start | bytes 393224 | tf_op jit(solution)/shard_map/ppermute | solution.py:206
  127.7 10.0 %collective-permute-start.12 = (bf16[1,32,2048]{2,1,0:T(8,128)(2,1)S(1)}, bf16[1,32,2048]{2,1,0:T(8,128)(2,1)S(1)}, u32[]{:S(2)}, u32[]{:S(2)}) collective-permute-start(bf16[1,32,2048]{2,1,0:T(8,128)(2,1)S(1)} %get-tuple-element.33), channel_id=1, source_target_pairs={{0,3},{1,2},{2,1},{3,0},{4,7},{5,6},{6,5},{7,4},{8,11},{9,10},{10,... | collective-permute-start | bytes 393224 | tf_op jit(solution)/shard_map/ppermute | solution.py:206
  129.2 12.0 %collective-permute-start.13 = (bf16[1,32,2048]{2,1,0:T(8,128)(2,1)S(1)}, bf16[1,32,2048]{2,1,0:T(8,128)(2,1)S(1)}, u32[]{:S(2)}, u32[]{:S(2)}) collective-permute-start(bf16[1,32,2048]{2,1,0:T(8,128)(2,1)S(1)} %get-tuple-element.32), channel_id=1, source_target_pairs={{0,4},{1,5},{2,6},{3,7},{4,0},{5,1},{6,2},{7,3},{8,12},{9,13},{10,... | collective-permute-start | bytes 393224 | tf_op jit(solution)/shard_map/ppermute | solution.py:206
  130.6 10.8 %collective-permute-start.14 = (bf16[1,32,2048]{2,1,0:T(8,128)(2,1)S(1)}, bf16[1,32,2048]{2,1,0:T(8,128)(2,1)S(1)}, u32[]{:S(2)}, u32[]{:S(2)}) collective-permute-start(bf16[1,32,2048]{2,1,0:T(8,128)(2,1)S(1)} %get-tuple-element.31), channel_id=1, source_target_pairs={{0,5},{1,4},{2,7},{3,6},{4,1},{5,0},{6,3},{7,2},{8,13},{9,12},{10,... | collective-permute-start | bytes 393224 | tf_op jit(solution)/shard_map/ppermute | solution.py:206
  131.0 55.4 %slice-start.1 = ((s8[5767168]{0:T(1024)(128)(4,1)}), s8[1572864]{0:T(1024)(128)(4,1)S(1)}, s32[]{:S(2)}) async-start(s8[5767168]{0:T(1024)(128)(4,1)} %bitcast.75), calls=%async_computation.4 | async-start | bytes 3145728
  134.9 9.2 %collective-permute-start.15 = (bf16[1,32,2048]{2,1,0:T(8,128)(2,1)S(1)}, bf16[1,32,2048]{2,1,0:T(8,128)(2,1)S(1)}, u32[]{:S(2)}, u32[]{:S(2)}) collective-permute-start(bf16[1,32,2048]{2,1,0:T(8,128)(2,1)S(1)} %get-tuple-element.30), channel_id=1, source_target_pairs={{0,6},{1,7},{2,4},{3,5},{4,2},{5,3},{6,0},{7,1},{8,14},{9,15},{10,... | collective-permute-start | bytes 393224 | tf_op jit(solution)/shard_map/ppermute | solution.py:206
  136.4 9.4 %collective-permute-start.16 = (bf16[1,32,2048]{2,1,0:T(8,128)(2,1)S(1)}, bf16[1,32,2048]{2,1,0:T(8,128)(2,1)S(1)}, u32[]{:S(2)}, u32[]{:S(2)}) collective-permute-start(bf16[1,32,2048]{2,1,0:T(8,128)(2,1)S(1)} %get-tuple-element.29), channel_id=1, source_target_pairs={{0,7},{1,6},{2,5},{3,4},{4,3},{5,2},{6,1},{7,0},{8,15},{9,14},{10,... | collective-permute-start | bytes 393224 | tf_op jit(solution)/shard_map/ppermute | solution.py:206
  137.8 20.3 %collective-permute-start.17 = (bf16[1,32,2048]{2,1,0:T(8,128)(2,1)S(1)}, bf16[1,32,2048]{2,1,0:T(8,128)(2,1)S(1)}, u32[]{:S(2)}, u32[]{:S(2)}) collective-permute-start(bf16[1,32,2048]{2,1,0:T(8,128)(2,1)S(1)} %get-tuple-element.28), channel_id=1, source_target_pairs={{0,8},{1,9},{2,10},{3,11},{4,12},{5,13},{6,14},{7,15},{8,0},{9,1},... | collective-permute-start | bytes 393224 | tf_op jit(solution)/shard_map/ppermute | solution.py:206
  141.2 19.7 %collective-permute-start.18 = (bf16[1,32,2048]{2,1,0:T(8,128)(2,1)S(1)}, bf16[1,32,2048]{2,1,0:T(8,128)(2,1)S(1)}, u32[]{:S(2)}, u32[]{:S(2)}) collective-permute-start(bf16[1,32,2048]{2,1,0:T(8,128)(2,1)S(1)} %get-tuple-element.27), channel_id=1, source_target_pairs={{0,9},{1,8},{2,11},{3,10},{4,13},{5,12},{6,15},{7,14},{8,1},{9,0},... | collective-permute-start | bytes 393224 | tf_op jit(solution)/shard_map/ppermute | solution.py:206
  141.4 27.8 %collective-permute-start.19 = (bf16[1,32,2048]{2,1,0:T(8,128)(2,1)S(1)}, bf16[1,32,2048]{2,1,0:T(8,128)(2,1)S(1)}, u32[]{:S(2)}, u32[]{:S(2)}) collective-permute-start(bf16[1,32,2048]{2,1,0:T(8,128)(2,1)S(1)} %get-tuple-element.26), channel_id=1, source_target_pairs={{0,10},{1,11},{2,8},{3,9},{4,14},{5,15},{6,12},{7,13},{8,2},{9,3},... | collective-permute-start | bytes 393224 | tf_op jit(solution)/shard_map/ppermute | solution.py:206
  144.1 28.1 %collective-permute-start.20 = (bf16[1,32,2048]{2,1,0:T(8,128)(2,1)S(1)}, bf16[1,32,2048]{2,1,0:T(8,128)(2,1)S(1)}, u32[]{:S(2)}, u32[]{:S(2)}) collective-permute-start(bf16[1,32,2048]{2,1,0:T(8,128)(2,1)S(1)} %get-tuple-element.25), channel_id=1, source_target_pairs={{0,11},{1,10},{2,9},{3,8},{4,15},{5,14},{6,13},{7,12},{8,3},{9,2},... | collective-permute-start | bytes 393224 | tf_op jit(solution)/shard_map/ppermute | solution.py:206
  145.8 29.1 %collective-permute-start.21 = (bf16[1,32,2048]{2,1,0:T(8,128)(2,1)S(1)}, bf16[1,32,2048]{2,1,0:T(8,128)(2,1)S(1)}, u32[]{:S(2)}, u32[]{:S(2)}) collective-permute-start(bf16[1,32,2048]{2,1,0:T(8,128)(2,1)S(1)} %get-tuple-element.24), channel_id=1, source_target_pairs={{0,12},{1,13},{2,14},{3,15},{4,8},{5,9},{6,10},{7,11},{8,4},{9,5},... | collective-permute-start | bytes 393224 | tf_op jit(solution)/shard_map/ppermute | solution.py:206
  158.1 23.5 %collective-permute-start.22 = (bf16[1,32,2048]{2,1,0:T(8,128)(2,1)S(1)}, bf16[1,32,2048]{2,1,0:T(8,128)(2,1)S(1)}, u32[]{:S(2)}, u32[]{:S(2)}) collective-permute-start(bf16[1,32,2048]{2,1,0:T(8,128)(2,1)S(1)} %get-tuple-element.23), channel_id=1, source_target_pairs={{0,13},{1,12},{2,15},{3,14},{4,9},{5,8},{6,11},{7,10},{8,5},{9,4},... | collective-permute-start | bytes 393224 | tf_op jit(solution)/shard_map/ppermute | solution.py:206
  160.9 22.6 %collective-permute-start.23 = (bf16[1,32,2048]{2,1,0:T(8,128)(2,1)S(1)}, bf16[1,32,2048]{2,1,0:T(8,128)(2,1)S(1)}, u32[]{:S(2)}, u32[]{:S(2)}) collective-permute-start(bf16[1,32,2048]{2,1,0:T(8,128)(2,1)S(1)} %get-tuple-element.22), channel_id=1, source_target_pairs={{0,14},{1,15},{2,12},{3,13},{4,10},{5,11},{6,8},{7,9},{8,6},{9,7},... | collective-permute-start | bytes 393224 | tf_op jit(solution)/shard_map/ppermute | solution.py:206
  169.2 17.1 %collective-permute-start.24 = (bf16[1,32,2048]{2,1,0:T(8,128)(2,1)S(1)}, bf16[1,32,2048]{2,1,0:T(8,128)(2,1)S(1)}, u32[]{:S(2)}, u32[]{:S(2)}) collective-permute-start(bf16[1,32,2048]{2,1,0:T(8,128)(2,1)S(1)} %get-tuple-element.21), channel_id=1, source_target_pairs={{0,15},{1,14},{2,13},{3,12},{4,11},{5,10},{6,9},{7,8},{8,7},{9,6},... | collective-permute-start | bytes 393224 | tf_op jit(solution)/shard_map/ppermute | solution.py:206
  193.0 6.2 %copy-start.5 = (f32[64,6]{0,1:T(8,128)S(1)}, f32[64,6]{0,1:T(8,128)}, u32[]{:S(2)}) copy-start(f32[64,6]{0,1:T(8,128)} %param.21) | copy-start | bytes 4612
  193.0 53.6 %all-to-all-start.2 = ((bf16[16,32,2048]{2,1,0:T(8,128)(2,1)}), bf16[16,32,2048]{2,1,0:T(8,128)(2,1)S(1)}, u32[]{:S(2)}, u32[]{:S(2)}) async-start(bf16[16,32,2048]{2,1,0:T(8,128)(2,1)} %bitcast.80), calls=%async_computation.2 | async-start | bytes 4194304 | tf_op jit(solution)/shard_map/all_to_all | solution.py:228
